TPU v7x, 32 devices: a whole 2x2x4 slice. The times are simulated.
32 devices in a mesh: section: 4 (over y, x), tp: 4 (over z), mirror: 2 (over core).
Axes of the slice: x: 2, y: 2, z: 4, core: 2. Of those that a mesh axis runs over, the one named last changes fastest.
Arguments:
- feats: bfloat16 [2, 2, 128, 5120], P('mirror', None, 'tp'), may hold values from -16 to 16
- types: int32 [2, 2, 128], P('mirror', None, 'tp'), may hold values from 0 to 63
- segs: int32 [2, 2, 5, 128], P('mirror'), may hold values from 0 to 3, never falling along the last dimension, each value on 1 to 64 neighbouring positions
- type_table: bfloat16 [64, 5120], replicated, may hold values from -3 to 3
- gains: float32 [2, 4, 5120], P('mirror', 'section'), may hold values from 0.25 to 1.75, as said below
- w_qkv: bfloat16 [2, 4, 3, 5120, 512], P('mirror', 'section', None, None, 'tp'), may hold values from -8 to 8, as said below
- w_out: bfloat16 [2, 4, 512, 5120], P('mirror', 'section', 'tp'), as said below
- carry_acts: bfloat16 [2, 4, 128, 5120], P('mirror', 'section', 'tp'), may hold values from -16 to 16
- grad_in: bfloat16 [2, 4, 128, 5120], P('mirror', 'section', 'tp'), may hold values from -6 to 6
- saved: bfloat16 [2, 4, 2, 128, 5120], P('mirror', 'section', None, 'tp'), may hold values from -16 to 16
- cotangent: bfloat16 [2, 2, 128, 5120], P('mirror', None, 'tp'), may hold values from -6 to 6
Outputs:
- acts: bfloat16 [2, 4, 2, 128, 5120], P('mirror', 'section', None, 'tp')
- grad_acts: bfloat16 [2, 4, 2, 128, 5120], P('mirror', 'section', None, 'tp')
- grad_qkv: bfloat16 [2, 4, 3, 5120, 512], P('mirror', 'section', None, None, 'tp')
- grad_out: bfloat16 [2, 4, 512, 5120], P('mirror', 'section', 'tp')
Inputs may be any that keep to these rules, and one draw needn't show every extreme that they name: w_qkv[1, k] equals w_qkv[0, 3 - k]. w_out[1, k] equals w_out[0, 3 - k]. gains[1, k] equals gains[0, 3 - k]. `segs`: segment numbers never fall along a micro-batch; each segment holds at most half of 128 tokens, and one holds exactly that many.
All inputs are finite; a program needn't handle non-finite values.
Results may differ from a plain program's by a relative error of at most 0.015.
Values may be sent and summed in bfloat16 or wider, within the bound.
No kernel may reach another device: no remote copies, remote signals or barrier semaphores. Data moves between devices by JAX's collectives and lax.ppermute only.
A program may use at most 128 MiB of HBM per device.

v0:
```python
import math
import numpy as np
import jax
import jax.numpy as jnp
from jax import lax
from jax.sharding import PartitionSpec as P

HD = 128


def passed_along(block, axis, distance):
    devices = range(lax.axis_size(axis))
    route = [(i - distance, i) for i in devices if i - distance in devices]
    return lax.ppermute(block, axis, route)


def flipped(value, axis, mask):
    return lax.ppermute(value, axis, [(i, i ^ mask) for i in range(lax.axis_size(axis))])


def normalize(values, gain_row):
    mean_square = jnp.mean(values * values, axis=-1, keepdims=True)
    return values * lax.rsqrt(mean_square + 1e-05) * gain_row


def segment_mask(segment_ids):
    position = jnp.arange(segment_ids.shape[0], dtype=jnp.int32)
    causal = position[None, :] <= position[:, None]
    return causal & (segment_ids[:, None] == segment_ids[None, :])


def attend(queries, keys_all, values_all, seg_mask):
    scores = jnp.einsum(
        "ihd,jhd->hij", queries, keys_all, preferred_element_type=jnp.float32
    ) / math.sqrt(queries.shape[-1])
    scores = jnp.where(seg_mask[None], scores, -1e30)
    highest = lax.stop_gradient(jnp.max(scores, axis=-1, keepdims=True))
    expo = jnp.exp(scores - highest)
    probs = (expo / jnp.sum(expo, axis=-1, keepdims=True)).astype(values_all.dtype)
    return jnp.einsum("hij,jhd->ihd", probs, values_all, preferred_element_type=jnp.float32)


def embedding(feat_rows, type_rows, type_table):
    onehot = (
        type_rows[:, None] == jnp.arange(type_table.shape[0], dtype=jnp.int32)[None, :]
    ).astype(jnp.bfloat16)
    looked = jnp.dot(onehot, type_table, preferred_element_type=jnp.float32)
    return (feat_rows.astype(jnp.float32) + looked).astype(jnp.bfloat16)


def gathered(blocks):
    full = lax.all_gather(jnp.stack(blocks), "tp", axis=1, tiled=True)
    return [full[i] for i in range(len(blocks))]


def scattered(blocks):
    part = lax.psum_scatter(jnp.stack(blocks), "tp", scatter_dimension=1, tiled=True)
    return [part[i] for i in range(len(blocks))]


def shards(
    feats, types, segs, type_table, gains, w_qkv, w_out, carry_acts, grad_in, saved, cotangent
):
    sections = lax.axis_size("section")
    section_index = lax.axis_index("section")
    on_first_pipe = lax.axis_index("mirror") == 0
    position = jnp.where(on_first_pipe, section_index, sections - 1 - section_index)
    gain_row = gains[0, 0]
    qkv_weight = w_qkv[0, 0]
    out_weight = w_out[0, 0]
    window_steps = feats.shape[1]
    seq_len = segs.shape[3]
    model_width = qkv_weight.shape[1]
    inner_here = qkv_weight.shape[-1]
    heads_here = inner_here // HD

    def mask_for(which, index):
        return segment_mask(lax.dynamic_index_in_dim(segs[0, which], index, 0, keepdims=False))

    def normed_rows(rows):
        return normalize(rows.astype(jnp.float32), gain_row).astype(jnp.bfloat16)

    def heads_of(normed_full):
        projected = jnp.einsum(
            "sd,cdn->csn", normed_full, qkv_weight, preferred_element_type=jnp.float32
        ).astype(jnp.bfloat16)
        return projected.reshape(3, seq_len, heads_here, HD)

    def forward_part(normed_full, seg_mask, heads_view=None):
        if heads_view is None:
            heads_view = heads_of(normed_full)
        mixed = (
            attend(heads_view[0], heads_view[1], heads_view[2], seg_mask)
            .reshape(seq_len, inner_here)
            .astype(jnp.bfloat16)
        )
        return mixed

    def backward_part(normed_full, upstream_full, seg_mask, heads_view=None):
        if heads_view is None:
            heads_view = heads_of(normed_full)
        primal, pull_attend = jax.vjp(
            lambda query_part, key_part, value_part: attend(
                query_part, key_part, value_part, seg_mask
            ),
            heads_view[0],
            heads_view[1],
            heads_view[2],
        )
        mixed = primal.reshape(seq_len, inner_here).astype(jnp.bfloat16)
        d_mixed = jnp.einsum(
            "sd,nd->sn", upstream_full, out_weight, preferred_element_type=jnp.float32
        ).astype(jnp.bfloat16)
        pulled = pull_attend(d_mixed.astype(jnp.float32).reshape(seq_len, heads_here, HD))
        d_projected = jnp.stack(pulled).reshape(3, seq_len, inner_here)
        return (d_projected, mixed)

    qkv_rows = jnp.transpose(qkv_weight, (0, 2, 1)).reshape(3 * inner_here, model_width)
    padded_out = jnp.concatenate(
        [out_weight, jnp.zeros((2 * inner_here, model_width), out_weight.dtype)], axis=0
    )
    block_weight = jnp.stack([qkv_rows, padded_out])

    def projected_back(d_projected, forward_mixed):
        lhs = jnp.stack(
            [
                jnp.transpose(d_projected, (1, 0, 2)).reshape(seq_len, 3 * inner_here),
                jnp.concatenate(
                    [forward_mixed, jnp.zeros((seq_len, 2 * inner_here), forward_mixed.dtype)],
                    axis=1,
                ),
            ]
        )
        return jnp.einsum(
            "tsk,tkd->tsd", lhs, block_weight, preferred_element_type=jnp.float32
        ).astype(jnp.bfloat16)

    def weight_terms(normed_fulls, d_projecteds, mixeds, upstream_fulls):
        qkv_sum = None
        out_sum = None
        for normed_full, d_projected, mixed, upstream_full in zip(
            normed_fulls, d_projecteds, mixeds, upstream_fulls
        ):
            qkv_term = jnp.einsum(
                "sd,csn->cdn", normed_full, d_projected, preferred_element_type=jnp.float32
            )
            out_term = jnp.einsum(
                "sn,sd->nd", mixed, upstream_full, preferred_element_type=jnp.float32
            )
            qkv_sum = qkv_term if qkv_sum is None else qkv_sum + qkv_term
            out_sum = out_term if out_sum is None else out_sum + out_term
        return (qkv_sum.astype(jnp.bfloat16), out_sum.astype(jnp.bfloat16))

    def input_grad(layer_in, upstream, d_normed):
        unused_norm, pull_norm = jax.vjp(
            lambda inputs: normalize(inputs, gain_row), layer_in.astype(jnp.float32)
        )
        d_input = pull_norm(d_normed.astype(jnp.float32))[0]
        return (upstream.astype(jnp.float32) + d_input).astype(jnp.bfloat16)

    pair_axes = ("section", "mirror")
    mirror_size = lax.axis_size("mirror")
    up_pairs = []
    down_pairs = []
    for section in range(sections):
        for mirror in range(mirror_size):
            ahead = 1 if mirror == 0 else -1
            if 0 <= section + ahead < sections:
                up_pairs.append(
                    (section * mirror_size + mirror, (section + ahead) * mirror_size + mirror)
                )
            if 0 <= section - ahead < sections:
                down_pairs.append(
                    (section * mirror_size + mirror, (section - ahead) * mirror_size + mirror)
                )
    bit_count = lax.axis_size(pair_axes).bit_length() - 1
    section_bits = list(range(1, bit_count))
    if section_bits:
        routes = []
        for start in range(len(section_bits)):
            order = section_bits[start:] + section_bits[:start]
            routes.append([1 | 1 << order[0]] + [1 << bit for bit in order[1:]])
    else:
        routes = [[1]]

    def to_partner(value):
        return flipped(value, pair_axes, (1 << bit_count) - 1)

    last_step = window_steps - 1
    saved_normed = [normed_rows(saved[0, 0, t]) for t in range(window_steps)]
    backward_normed_full = [None] * window_steps
    upstream_fulls = []
    d_projecteds = []
    mixeds = []
    partner_normed = [None] * window_steps
    partner_upstream = []
    partner_d_projected = []
    partner_mixed = []
    forward_outs = []
    backward_outs = []
    forward_in = carry_acts[0, 0]
    backward_in = grad_in[0, 0]
    inbox = {}
    deferred = {}
    tie_scatter = {}
    for step_index in range(window_steps):
        embedded = embedding(feats[0, step_index], types[0, step_index], type_table)
        current = jnp.where(position == 0, embedded, forward_in)
        upstream = jnp.where(position == sections - 1, cotangent[0, step_index], backward_in)
        if step_index == 0:
            upstream_full, backward_normed_full[0], forward_normed_full = gathered(
                [upstream, saved_normed[0], normed_rows(current)]
            )
            first_sent = to_partner(jnp.stack([upstream_full, backward_normed_full[0]]))
            paired = jnp.einsum(
                "tsd,cdn->tcsn",
                jnp.stack([backward_normed_full[0], forward_normed_full]),
                qkv_weight,
                preferred_element_type=jnp.float32,
            ).astype(jnp.bfloat16)
            step_heads = [paired[t].reshape(3, seq_len, heads_here, HD) for t in range(2)]
        else:
            step_heads = [None, None]
            upstream_full, forward_normed_full = gathered([upstream, normed_rows(current)])
            inbox[f"rows{step_index}"] = to_partner(upstream_full)
        d_projected, mixed = backward_part(
            backward_normed_full[step_index],
            upstream_full,
            mask_for(1, step_index + position),
            step_heads[0],
        )
        upstream_fulls.append(upstream_full)
        d_projecteds.append(d_projected)
        mixeds.append(mixed)
        small = jnp.concatenate([d_projected, mixed[None]])
        if step_index < last_step:
            deferred[f"small{step_index}"] = small
        else:
            inbox[f"small{step_index}"] = to_partner(small)
        forward_mixed = forward_part(
            forward_normed_full, mask_for(0, step_index - position + sections - 1), step_heads[1]
        )
        both_parts, tie_scatter = lax.optimization_barrier(
            (projected_back(d_projected, forward_mixed), tie_scatter)
        )
        inbox.update(tie_scatter)
        tie_scatter = {}
        both_rows = lax.psum_scatter(both_parts, "tp", scatter_dimension=1, tiled=True)
        d_normed, attn_rows = (both_rows[0], both_rows[1])
        if step_index == 0 and window_steps > 1:
            later_rows, d_normed = lax.optimization_barrier((saved_normed[1:], d_normed))
            later = gathered(later_rows)
            backward_normed_full[1:] = later
            deferred["later"] = jnp.stack(later)
        backward_out = input_grad(saved[0, 0, step_index], upstream, d_normed)
        forward_out = (current.astype(jnp.float32) + attn_rows.astype(jnp.float32)).astype(
            jnp.bfloat16
        )
        forward_outs.append(forward_out)
        backward_outs.append(backward_out)
        if step_index < last_step:
            backward_in = lax.ppermute(backward_out, pair_axes, down_pairs)
            forward_in = lax.ppermute(forward_out, pair_axes, up_pairs)
            if step_index == 0:
                deferred, first_sent, backward_in, forward_in = lax.optimization_barrier(
                    (deferred, first_sent, backward_in, forward_in)
                )
                inbox["first"] = first_sent
            else:
                deferred, backward_in, forward_in = lax.optimization_barrier(
                    (deferred, backward_in, forward_in)
                )
            tie_scatter = {key: to_partner(value) for key, value in deferred.items()}
            deferred = {}
    partner_upstream = [inbox["first"][0]] + [inbox[f"rows{t}"] for t in range(1, window_steps)]
    partner_normed = [inbox["first"][1]] + (
        [inbox["later"][t] for t in range(window_steps - 1)] if window_steps > 1 else []
    )
    partner_d_projected = [inbox[f"small{t}"][:3] for t in range(window_steps)]
    partner_mixed = [inbox[f"small{t}"][3] for t in range(window_steps)]
    own_qkv, own_out = weight_terms(backward_normed_full, d_projecteds, mixeds, upstream_fulls)
    other_qkv, other_out = weight_terms(
        partner_normed, partner_d_projected, partner_mixed, partner_upstream
    )
    grad_qkv = (own_qkv.astype(jnp.float32) + other_qkv.astype(jnp.float32)).astype(jnp.bfloat16)
    grad_out = (own_out.astype(jnp.float32) + other_out.astype(jnp.float32)).astype(jnp.bfloat16)
    acts_block = jnp.stack(forward_outs)[None, None]
    grads_block = jnp.stack(backward_outs)[None, None]
    return (acts_block, grads_block, grad_qkv[None, None], grad_out[None, None])


def solution(mesh):
    in_specs = (
        P("mirror", None, "tp", None),
        P("mirror", None, "tp"),
        P("mirror", None, None, None),
        P(),
        P("mirror", "section", None),
        P("mirror", "section", None, None, "tp"),
        P("mirror", "section", "tp", None),
        P("mirror", "section", "tp", None),
        P("mirror", "section", "tp", None),
        P("mirror", "section", None, "tp", None),
        P("mirror", None, "tp", None),
    )
    out_specs = (
        P("mirror", "section", None, "tp", None),
        P("mirror", "section", None, "tp", None),
        P("mirror", "section", None, None, "tp"),
        P("mirror", "section", "tp", None),
    )
    return jax.shard_map(shards, mesh=mesh, in_specs=in_specs, out_specs=out_specs, check_vma=False)
```

profile of v0, /device:TPU:0, one launch (start us, length us, event | category | flops | bytes accessed | tf_op | source)
XLA Modules:
  0.0 318.5 jit_solution(18364899609434030031)
XLA Ops:
  13.8 6.3 %copy.15 = bf16[3,128,5120]{2,1,0:T(8,128)(2,1)} copy(bf16[3,128,5120]{1,2,0:T(8,128)(2,1)} %bitcast.361) | data formatting | bytes 7864320 | tf_op jit(solution)/shard_map/transpose | solution.py:118
  20.6 3.7 %pad_bitcast_fusion = bf16[1,384,5120]{2,1,0:T(8,128)(2,1)} fusion(bf16[128,5120]{1,0:T(8,128)(2,1)} %bitcast.363), kind=kLoop, calls=%fused_computation.28 | loop fusion | bytes 5242880 | tf_op jit(solution)/shard_map/stack | solution.py:122
  24.3 68.7 %all-gather.5.cloned.1.call-done = bf16[3,128,5120]{2,1,0:T(8,128)(2,1)} async-done(((bf16[3,32,5120]{2,1,0:T(8,128)(2,1)}), bf16[3,128,5120]{2,1,0:T(8,128)(2,1)}) %all-gather.5.cloned.1.call-update) | async-done | bytes 3932176 | tf_op jit(solution)/shard_map/all_gather | solution.py:52
  93.0 4.6 %fusion.33 = bf16[2,3,128,128]{3,2,1,0:T(8,128)(2,1)S(1)} fusion(bf16[1,1,3,5120,128]{4,3,2,1,0:T(8,128)(2,1)} %param.16, bf16[3,128,5120]{2,1,0:T(8,128)(2,1)} %all-gather.5.cloned.1.call-done), kind=kOutput, calls=%fused_computation.47 | convolution fusion | flops 1006731264 | bytes 6750208 | tf_op jit(solution)/shard_map/tsd,cdn->tcsn/dot_general | solution.py:215
  97.9 2.0 fusion.68
  101.3 3.0 convolution_convert_fusion.1
  105.6 3.5 %stack.115 = bf16[2,128,5120]{2,1,0:T(8,128)(2,1)} slice(bf16[3,128,5120]{2,1,0:T(8,128)(2,1)} %all-gather.5.cloned.1.call-done), slice={[0:2], [0:128], [0:5120]} | slice | bytes 5242880 | tf_op jit(solution)/shard_map/stack | solution.py:214
  110.8 44.5 %reduce-scatter.3.cloned.1.call-done = bf16[2,32,5120]{2,1,0:T(8,128)(2,1)} async-done(((bf16[2,128,5120]{2,1,0:T(8,128)(2,1)}), bf16[2,32,5120]{2,1,0:T(8,128)(2,1)}) %reduce-scatter.3.cloned.1.call-update) | async-done | bytes 655376 | tf_op jit(solution)/shard_map/reduce_scatter | solution.py:248
  159.2 5.3 %collective-permute-start.2 = (bf16[32,5120]{1,0:T(8,128)(2,1)S(1)}, bf16[32,5120]{1,0:T(8,128)(2,1)}, u32[]{:S(2)}, u32[]{:S(2)}) collective-permute-start(bf16[32,5120]{1,0:T(8,128)(2,1)S(1)} %fusion.90), channel_id=1, source_target_pairs={{0,8},{8,16},{9,1},{16,24},{17,9},{25,17},{2,10},{10,18},{11,3},{1... | collective-permute-start | bytes 983048 | tf_op jit(solution)/shard_map/ppermute | solution.py:263
  166.1 3.3 %collective-permute-done = bf16[2,128,5120]{2,1,0:T(8,128)(2,1)} collective-permute-done((bf16[2,128,5120]{2,1,0:T(8,128)(2,1)}, bf16[2,128,5120]{2,1,0:T(8,128)(2,1)}, u32[]{:S(2)}, u32[]{:S(2)}) %collective-permute-start) | collective-permute-done | bytes 2621472 | tf_op jit(solution)/shard_map/ppermute | solution.py:18
  169.4 6.7 %collective-permute-done.1 = bf16[32,5120]{1,0:T(8,128)(2,1)S(1)} collective-permute-done((bf16[32,5120]{1,0:T(8,128)(2,1)S(1)}, bf16[32,5120]{1,0:T(8,128)(2,1)S(1)}, u32[]{:S(2)}, u32[]{:S(2)}) %collective-permute-start.1) | collective-permute-done | bytes 327712 | tf_op jit(solution)/shard_map/ppermute | solution.py:262
  176.1 13.3 %all-gather.9.cloned.1.call-done = bf16[128,5120]{1,0:T(8,128)(2,1)} async-done(((bf16[32,5120]{1,0:T(8,128)(2,1)}), bf16[128,5120]{1,0:T(8,128)(2,1)}) %all-gather.9.cloned.1.call-update) | async-done | bytes 1310736 | tf_op jit(solution)/shard_map/all_gather | solution.py:52
  193.8 3.0 fusion.44
  197.0 48.9 %all-gather.7.cloned.1.call-done = bf16[2,128,5120]{2,1,0:T(8,128)(2,1)} async-done(((bf16[2,32,5120]{2,1,0:T(8,128)(2,1)}), bf16[2,128,5120]{2,1,0:T(8,128)(2,1)}) %all-gather.7.cloned.1.call-update) | async-done | bytes 2621456 | tf_op jit(solution)/shard_map/all_gather | solution.py:52
  248.1 3.5 %fusion.49 = bf16[3,128,128]{2,1,0:T(8,128)(2,1)S(1)} fusion(bf16[1,1,3,5120,128]{4,3,2,1,0:T(8,128)(2,1)} %param.16, bf16[2,128,5120]{2,1,0:T(8,128)(2,1)} %all-gather.7.cloned.1.call-done), kind=kOutput, calls=%fused_computation.55 | convolution fusion | flops 503365632 | bytes 5341184 | tf_op jit(solution)/shard_map/sd,cdn->csn/dot_general | solution.py:84
  252.9 3.0 convolution_convert_fusion
  258.5 2.6 fusion.18
  266.9 3.4 %fusion.19 = f32[128,5120]{1,0:T(8,128)} fusion(bf16[2,128,5120]{2,1,0:T(8,128)(2,1)} %collective-permute-done, bf16[4,128,128]{1,2,0:T(8,128)(2,1)S(1)} %collective-permute-done.4), kind=kOutput, calls=%fused_computation.35 | convolution fusion | flops 167772160 | bytes 3964928 | tf_op jit(solution)/shard_map/sn,sd->nd/dot_general | solution.py:147
  270.3 2.5 fusion.21
  272.8 4.4 %fusion = bf16[1,1,3,5120,128]{3,4,2,1,0:T(8,128)(2,1)} fusion(f32[3,128,5120]{2,1,0:T(8,128)S(1)} %fusion.21, bf16[4,128,128]{1,2,0:T(8,128)(2,1)S(1)} %collective-permute-done.4, bf16[3,128,5120]{2,1,0:T(8,128)(2,1)S(1)} %add_convert_fusion.2, bf16[2,128,5120]{2,1,0:T(8,128)(2,1)} %collective-permute-done), kind=kOutput, calls=%fused_computation.6 | convolution fusion | flops 515112960 | bytes 17170432 | tf_op jit(solution)/shard_map/sd,csn->cdn/dot_general | solution.py:144
  277.3 6.3 %copy.18 = bf16[1,1,3,5120,128]{4,3,2,1,0:T(8,128)(2,1)} copy(bf16[1,1,3,5120,128]{3,4,2,1,0:T(8,128)(2,1)} %fusion) | data formatting | bytes 7864320
  283.5 11.9 %collective-permute-done.6 = bf16[128,5120]{1,0:T(8,128)(2,1)} collective-permute-done((bf16[128,5120]{1,0:T(8,128)(2,1)}, bf16[128,5120]{1,0:T(8,128)(2,1)}, u32[]{:S(2)}, u32[]{:S(2)}) %collective-permute-start.6) | collective-permute-done | bytes 1310752 | tf_op jit(solution)/shard_map/ppermute | solution.py:18
  295.4 3.8 %fusion.7 = bf16[1,1,128,5120]{3,2,1,0:T(8,128)(2,1)} fusion(f32[128,5120]{1,0:T(8,128)S(1)} %fusion.6, f32[128,5120]{1,0:T(8,128)} %fusion.19, bf16[128,5120]{1,0:T(8,128)(2,1)} %collective-permute-done.6, bf16[4,128,128]{1,2,0:T(8,128)(2,1)S(1)} %collective-permute-done.5), kind=kOutput, calls=%fused_computation.15 | convolution fusion | flops 171048960 | bytes 7897088 | tf_op jit(solution)/shard_map/sn,sd->nd/dot_general | solution.py:147
  299.2 7.9 %reduce-scatter.5.cloned.1.call-done = bf16[2,32,5120]{2,1,0:T(8,128)(2,1)} async-done(((bf16[2,128,5120]{2,1,0:T(8,128)(2,1)}), bf16[2,32,5120]{2,1,0:T(8,128)(2,1)}) %reduce-scatter.5.cloned.1.call-update) | async-done | bytes 655376 | tf_op jit(solution)/shard_map/reduce_scatter | solution.py:248
  (142 shorter events, 38.1 us)
Async XLA Ops:
  7.2 85.8 %all-gather.5.cloned.1.call-start = ((), (), s32[]{:S(2)}) async-start(), calls=%async_computation.2 | async-start | bytes 4915200 | tf_op jit(solution)/shard_map/all_gather | solution.py:52
  13.7 141.5 %reduce-scatter.3.cloned.1.call-start = ((), (), s32[]{:S(2)}) async-start(), calls=%async_computation.3 | async-start | bytes 3276800 | tf_op jit(solution)/shard_map/reduce_scatter | solution.py:248
  13.8 6.3 %copy-start.27 = (s32[1,2,5,128]{3,1,2,0:T(2,128)S(1)}, s32[1,2,5,128]{3,1,2,0:T(2,128)}, u32[]{:S(2)}) copy-start(s32[1,2,5,128]{3,1,2,0:T(2,128)} %param.13) | copy-start | bytes 15364
  93.0 8.3 %copy-start.4 = (bf16[1,384,5120]{2,1,0:T(8,128)(2,1)S(1)}, bf16[1,384,5120]{2,1,0:T(8,128)(2,1)}, u32[]{:S(2)}) copy-start(bf16[1,384,5120]{2,1,0:T(8,128)(2,1)} %pad_bitcast_fusion) | copy-start | bytes 11796484
  104.3 85.2 %all-gather.9.cloned.1.call-start = ((), (), s32[]{:S(2)}) async-start(), calls=%async_computation.6 | async-start | bytes 1638400 | tf_op jit(solution)/shard_map/all_gather | solution.py:52
  109.1 60.3 %collective-permute-start = (bf16[2,128,5120]{2,1,0:T(8,128)(2,1)}, bf16[2,128,5120]{2,1,0:T(8,128)(2,1)}, u32[]{:S(2)}, u32[]{:S(2)}) collective-permute-start(bf16[2,128,5120]{2,1,0:T(8,128)(2,1)} %stack.115), channel_id=1, source_target_pairs={{0,25},{1,24},{8,17},{9,16},{16,9},{17,8},{24,1},{25,0},{2,27},{3,... | collective-permute-start | bytes 7864328 | tf_op jit(solution)/shard_map/ppermute | solution.py:18
  156.3 89.7 %all-gather.7.cloned.1.call-start = ((), (), s32[]{:S(2)}) async-start(), calls=%async_computation.4 | async-start | bytes 3276800 | tf_op jit(solution)/shard_map/all_gather | solution.py:52
  156.8 32.9 %copy-start.18 = (bf16[32,5120]{1,0:T(8,128)(2,1)}, bf16[32,5120]{1,0:T(8,128)(2,1)S(1)}, u32[]{:S(2)}) copy-start(bf16[32,5120]{1,0:T(8,128)(2,1)S(1)} %fusion.78) | copy-start | bytes 983044
  156.9 19.3 %collective-permute-start.1 = (bf16[32,5120]{1,0:T(8,128)(2,1)S(1)}, bf16[32,5120]{1,0:T(8,128)(2,1)S(1)}, u32[]{:S(2)}, u32[]{:S(2)}) collective-permute-start(bf16[32,5120]{1,0:T(8,128)(2,1)S(1)} %fusion.78), channel_id=1, source_target_pairs={{1,9},{8,0},{9,17},{16,8},{17,25},{24,16},{3,11},{10,2},{11,19},{1... | collective-permute-start | bytes 983048 | tf_op jit(solution)/shard_map/ppermute | solution.py:262
  159.2 30.3 %copy-start.15 = (bf16[32,5120]{1,0:T(8,128)(2,1)}, bf16[32,5120]{1,0:T(8,128)(2,1)S(1)}, u32[]{:S(2)}) copy-start(bf16[32,5120]{1,0:T(8,128)(2,1)S(1)} %fusion.90) | copy-start | bytes 983044
  159.2 16.9 %collective-permute-start.2 = (bf16[32,5120]{1,0:T(8,128)(2,1)S(1)}, bf16[32,5120]{1,0:T(8,128)(2,1)}, u32[]{:S(2)}, u32[]{:S(2)}) collective-permute-start(bf16[32,5120]{1,0:T(8,128)(2,1)S(1)} %fusion.90), channel_id=1, source_target_pairs={{0,8},{8,16},{9,1},{16,24},{17,9},{25,17},{2,10},{10,18},{11,3},{1... | collective-permute-start | bytes 983048 | tf_op jit(solution)/shard_map/ppermute | solution.py:263
  165.4 10.7 %copy-start.24 = (bf16[128,128]{1,0:T(8,128)(2,1)}, bf16[128,128]{1,0:T(8,128)(2,1)S(1)}, u32[]{:S(2)}) copy-start(bf16[128,128]{1,0:T(8,128)(2,1)S(1)} %convolution_convert_fusion.8) | copy-start | bytes 98308
  176.1 14.7 %copy-start.20 = (bf16[32,5120]{1,0:T(8,128)(2,1)}, bf16[32,5120]{1,0:T(8,128)(2,1)S(1)}, u32[]{:S(2)}) copy-start(bf16[32,5120]{1,0:T(8,128)(2,1)S(1)} %collective-permute-done.1) | copy-start | bytes 983044
  189.7 7.1 %copy-start.10 = (bf16[32,5120]{1,0:T(8,128)(2,1)}, bf16[32,5120]{1,0:T(8,128)(2,1)S(1)}, u32[]{:S(2)}) copy-start(bf16[32,5120]{1,0:T(8,128)(2,1)S(1)} %get-tuple-element.31) | copy-start | bytes 983044
  190.9 55.1 %copy-start.14 = (bf16[1,1,128,5120]{3,2,1,0:T(8,128)(2,1)S(1)}, bf16[1,1,128,5120]{3,2,1,0:T(8,128)(2,1)}, u32[]{:S(2)}) copy-start(bf16[1,1,128,5120]{3,2,1,0:T(8,128)(2,1)} %param.17) | copy-start | bytes 3932164
  190.9 116.2 %reduce-scatter.5.cloned.1.call-start = ((), (), s32[]{:S(2)}) async-start(), calls=%async_computation.5 | async-start | bytes 3276800 | tf_op jit(solution)/shard_map/reduce_scatter | solution.py:248
  191.1 64.8 %collective-permute-start.3 = (bf16[1,128,5120]{2,1,0:T(8,128)(2,1)S(1)}, bf16[1,128,5120]{2,1,0:T(8,128)(2,1)}, u32[]{:S(2)}, u32[]{:S(2)}) collective-permute-start(bf16[1,128,5120]{2,1,0:T(8,128)(2,1)S(1)} %bitcast.362), channel_id=1, source_target_pairs={{0,25},{1,24},{8,17},{9,16},{16,9},{17,8},{24,1},{25,0},{2,27},{3,... | collective-permute-start | bytes 3932168 | tf_op jit(solution)/shard_map/ppermute | solution.py:18
  192.3 63.6 %collective-permute-start.4 = (bf16[4,128,128]{1,2,0:T(8,128)(2,1)}, bf16[4,128,128]{1,2,0:T(8,128)(2,1)S(1)}, u32[]{:S(2)}, u32[]{:S(2)}) collective-permute-start(bf16[4,128,128]{1,2,0:T(8,128)(2,1)} %pad_maximum_fusion.5), channel_id=1, source_target_pairs={{0,25},{1,24},{8,17},{9,16},{16,9},{17,8},{24,1},{25,0},{2,27},{3,... | collective-permute-start | bytes 393224 | tf_op jit(solution)/shard_map/ppermute | solution.py:18
  246.0 6.9 %copy-start.5 = (bf16[1,384,5120]{2,1,0:T(8,128)(2,1)S(1)}, bf16[1,384,5120]{2,1,0:T(8,128)(2,1)}, u32[]{:S(2)}) copy-start(bf16[1,384,5120]{2,1,0:T(8,128)(2,1)} %pad_bitcast_fusion) | copy-start | bytes 11796484
  261.3 9.0 %collective-permute-start.5 = (bf16[4,128,128]{1,2,0:T(8,128)(2,1)S(1)}, bf16[4,128,128]{1,2,0:T(8,128)(2,1)S(1)}, u32[]{:S(2)}, u32[]{:S(2)}) collective-permute-start(bf16[4,128,128]{1,2,0:T(8,128)(2,1)S(1)} %pad_maximum_fusion.6), channel_id=1, source_target_pairs={{0,25},{1,24},{8,17},{9,16},{16,9},{17,8},{24,1},{25,0},{2,27},{3,... | collective-permute-start | bytes 393224 | tf_op jit(solution)/shard_map/ppermute | solution.py:18
  264.2 31.3 %collective-permute-start.6 = (bf16[128,5120]{1,0:T(8,128)(2,1)}, bf16[128,5120]{1,0:T(8,128)(2,1)}, u32[]{:S(2)}, u32[]{:S(2)}) collective-permute-start(bf16[128,5120]{1,0:T(8,128)(2,1)} %slice_bitcast_fusion.6), channel_id=1, source_target_pairs={{0,25},{1,24},{8,17},{9,16},{16,9},{17,8},{24,1},{25,0},{2,27},{3,... | collective-permute-start | bytes 3932168 | tf_op jit(solution)/shard_map/ppermute | solution.py:18
  283.5 23.6 %copy-start.7 = (bf16[1,1,2,32,5120]{4,3,2,1,0:T(8,128)(2,1)S(1)}, bf16[1,1,2,32,5120]{4,3,2,1,0:T(8,128)(2,1)}, u32[]{:S(2)}) copy-start(bf16[1,1,2,32,5120]{4,3,2,1,0:T(8,128)(2,1)} %param.20) | copy-start | bytes 1966084
  299.2 11.0 %copy-start.19 = (bf16[32,5120]{1,0:T(8,128)(2,1)S(1)}, bf16[32,5120]{1,0:T(8,128)(2,1)}, u32[]{:S(2)}) copy-start(bf16[32,5120]{1,0:T(8,128)(2,1)} %copy-done.18) | copy-start | bytes 983044
  299.2 11.9 %copy-start.16 = (bf16[32,5120]{1,0:T(8,128)(2,1)S(1)}, bf16[32,5120]{1,0:T(8,128)(2,1)}, u32[]{:S(2)}) copy-start(bf16[32,5120]{1,0:T(8,128)(2,1)} %copy-done.15) | copy-start | bytes 983044
  (17 other events, 58.8 us)
Sparse Core Ops, SparseCore 0:
  13.8 79.1 all-gather.4
  104.4 50.7 reduce-scatter.2
  157.4 32.0 all-gather.8
  191.5 54.4 all-gather.6
  256.0 51.0 reduce-scatter.4
where the time goes:
time: 320 us; the launch traced here: 319 us
  waiting for transfers between devices  205 us (64%)
  matrix products  47.8 us (15%)
  local copies, waits for them, and re-layouts  24.6 us (8%)
  between operations  14.4 us (4%)
  starting transfers between devices  14.1 us (4%)
  other arithmetic  12.3 us (4%)
    all_gather x3, waiting for transfers between devices, gathered(): full = lax.all_gather(jnp.stack(blocks), 'tp', axis=1, tiled=True)  131 us
    reduce_scatter x2, waiting for transfers between devices, shards(): lax.psum_scatter(both_parts, 'tp', scatter_dimension=1, tiled=True)  52.4 us
    ppermute x5, waiting for transfers between devices, flipped(): lax.ppermute(value, axis, [(i, i ^ mask) for i in range(lax.axis_size(axi...  15.3 us
    dot_general x4, matrix products, weight_terms(): jnp.einsum('sd,csn->cdn', normed_full, d_projected, preferred_element_typ...  10.7 us
    dot_general x4, matrix products, weight_terms(): jnp.einsum('sn,sd->nd', mixed, upstream_full, preferred_element_type=jnp....  9.49 us
    unnamed x59, local copies, waits for them, and re-layouts  7.12 us
    ppermute x5, starting transfers between devices, flipped(): lax.ppermute(value, axis, [(i, i ^ mask) for i in range(lax.axis_size(axi...  7.08 us
    ppermute x1, waiting for transfers between devices, shards(): backward_in = lax.ppermute(backward_out, pair_axes, down_pairs)  6.69 us
  transfers between devices with their start and end apart: 12, of which 8 were waited for; matrix products, arithmetic and copies ran while one was open for 19% of the time, Pallas kernels for 0%

commit v1 on v0

--- a/solution.py
+++ b/solution.py
@@ -49,7 +49,22 @@
 
 
 def gathered(blocks):
-    full = lax.all_gather(jnp.stack(blocks), "tp", axis=1, tiled=True)
+    x = jnp.stack(blocks)
+    ways, here, step = (lax.axis_size("tp"), lax.axis_index("tp"), x.shape[1])
+    lengths = [n * ways if d == 1 else n for d, n in enumerate(x.shape)]
+    full_2 = lax.dynamic_update_slice_in_dim(jnp.zeros(lengths, x.dtype), x, here * step, axis=1)
+    going_up = going_down = x
+    for far in range(1, ways // 2 + 1):
+        going_up = lax.ppermute(going_up, "tp", [(d, (d + 1) % ways) for d in range(ways)])
+        full_2 = lax.dynamic_update_slice_in_dim(
+            full_2, going_up, (here - far) % ways * step, axis=1
+        )
+        if 2 * far < ways:
+            going_down = lax.ppermute(going_down, "tp", [(d, (d - 1) % ways) for d in range(ways)])
+            full_2 = lax.dynamic_update_slice_in_dim(
+                full_2, going_down, (here + far) % ways * step, axis=1
+            )
+    full = full_2
     return [full[i] for i in range(len(blocks))]
 
 

time: 320 us -> 292 us (0.912)
  waiting for transfers between devices: 205 us -> 147 us
  starting transfers between devices: 14.1 us -> 44 us
  local copies, waits for them, and re-layouts: 24.6 us -> 35.5 us
  matrix products: 47.8 us -> 37.2 us
    all_gather x3 -> x0, waiting for transfers between devices: 131 us -> none  [gathered(): full = lax.all_gather(jnp.stack(blocks), 'tp', axis=1, tiled=True)]
    ppermute x0 -> x9, waiting for transfers between devices: none -> 82.2 us  [the longest x6 67.3 us: gathered(): lax.ppermute(going_up, 'tp', [(d, (d + 1) % ways) for d in range(ways)])]
    ppermute x0 -> x9, starting transfers between devices: none -> 33 us  [the longest x6 25.2 us: gathered(): lax.ppermute(going_up, 'tp', [(d, (d + 1) % ways) for d in range(ways)])]
    dynamic_update_slice x0 -> x10, local copies, waits for them, and re-layouts: none -> 6.78 us  [the longest x6 3.48 us: gathered(): lax.dynamic_update_slice_in_dim(full_2, going_up, (here - far) % ways * s...]
    ppermute x1, waiting for transfers between devices: 6.69 us -> 0.01 us  [shards(): backward_in = lax.ppermute(backward_out, pair_axes, down_pairs)]
    ppermute x5, waiting for transfers between devices: 15.3 us -> 10.3 us  [flipped(): lax.ppermute(value, axis, [(i, i ^ mask) for i in range(lax.axis_size(axi...]
    dot_general x2, matrix products: 6.45 us -> 1.72 us  [heads_of(): jnp.einsum('sd,cdn->csn', normed_full, qkv_weight, preferred_element_type...]
    unnamed x59 -> x77, local copies, waits for them, and re-layouts: 7.12 us -> 10.5 us
  transfers between devices with their start and end apart: 12 -> 18, of which waited for: 8 -> 11; matrix products, arithmetic and copies ran while one was open for 19% -> 19% of each run, Pallas kernels for 0% -> 0%
where the time goes in v1:
time: 292 us; the launch traced here: 291 us
  waiting for transfers between devices  147 us (50%)
  starting transfers between devices  44 us (15%)
  matrix products  37.2 us (13%)
  local copies, waits for them, and re-layouts  35.5 us (12%)
  between operations  14.9 us (5%)
  other arithmetic  12.6 us (4%)
    ppermute x6, waiting for transfers between devices, gathered(): lax.ppermute(going_up, 'tp', [(d, (d + 1) % ways) for d in range(ways)])  67.3 us
    reduce_scatter x2, waiting for transfers between devices, shards(): lax.psum_scatter(both_parts, 'tp', scatter_dimension=1, tiled=True)  54.5 us
    ppermute x6, starting transfers between devices, gathered(): lax.ppermute(going_up, 'tp', [(d, (d + 1) % ways) for d in range(ways)])  25.2 us
    ppermute x3, waiting for transfers between devices, gathered(): lax.ppermute(going_down, 'tp', [(d, (d - 1) % ways) for d in range(ways)])  14.9 us
    unnamed x77, local copies, waits for them, and re-layouts  10.5 us
    ppermute x5, waiting for transfers between devices, flipped(): lax.ppermute(value, axis, [(i, i ^ mask) for i in range(lax.axis_size(axi...  10.3 us
    dot_general x4, matrix products, weight_terms(): jnp.einsum('sd,csn->cdn', normed_full, d_projected, preferred_element_typ...  9.37 us
    dot_general x4, matrix products, weight_terms(): jnp.einsum('sn,sd->nd', mixed, upstream_full, preferred_element_type=jnp....  8.84 us
  transfers between devices with their start and end apart: 18, of which 11 were waited for; matrix products, arithmetic and copies ran while one was open for 19% of the time, Pallas kernels for 0%

profile of v1, /device:TPU:0, one launch (start us, length us, event | category | flops | bytes accessed | tf_op | source)
XLA Modules:
  0.0 291.2 jit_solution(2449387656435051768)
XLA Ops:
  16.9 3.0 %collective-permute-start = (bf16[3,32,5120]{2,1,0:T(8,128)(2,1)}, bf16[3,32,5120]{2,1,0:T(8,128)(2,1)}, u32[]{:S(2)}, u32[]{:S(2)}) collective-permute-start(bf16[3,32,5120]{2,1,0:T(8,128)(2,1)} %get-tuple-element.32), channel_id=1, source_target_pairs={{0,2},{2,4},{4,6},{6,0},{1,3},{3,5},{5,7},{7,1},{8,10},{10,12},{12... | collective-permute-start | bytes 2949128 | tf_op jit(solution)/shard_map/ppermute | solution.py:58
  22.0 6.5 %copy.15 = bf16[3,128,5120]{2,1,0:T(8,128)(2,1)} copy(bf16[3,128,5120]{1,2,0:T(8,128)(2,1)} %bitcast.363) | data formatting | bytes 7864320 | tf_op jit(solution)/shard_map/transpose | solution.py:133
  29.0 16.0 %collective-permute-done = bf16[3,32,5120]{2,1,0:T(8,128)(2,1)} collective-permute-done((bf16[3,32,5120]{2,1,0:T(8,128)(2,1)}, bf16[3,32,5120]{2,1,0:T(8,128)(2,1)}, u32[]{:S(2)}, u32[]{:S(2)}) %collective-permute-start) | collective-permute-done | bytes 983072 | tf_op jit(solution)/shard_map/ppermute | solution.py:58
  45.0 16.6 %collective-permute-start.2 = (bf16[3,32,5120]{2,1,0:T(8,128)(2,1)}, bf16[3,32,5120]{2,1,0:T(8,128)(2,1)S(1)}, u32[]{:S(2)}, u32[]{:S(2)}) collective-permute-start(bf16[3,32,5120]{2,1,0:T(8,128)(2,1)} %collective-permute-done), channel_id=1, source_target_pairs={{0,2},{2,4},{4,6},{6,0},{1,3},{3,5},{5,7},{7,1},{8,10},{10,12},{12... | collective-permute-start | bytes 2949128 | tf_op jit(solution)/shard_map/ppermute | solution.py:58
  67.0 18.2 %collective-permute-done.2 = bf16[3,32,5120]{2,1,0:T(8,128)(2,1)S(1)} collective-permute-done((bf16[3,32,5120]{2,1,0:T(8,128)(2,1)}, bf16[3,32,5120]{2,1,0:T(8,128)(2,1)S(1)}, u32[]{:S(2)}, u32[]{:S(2)}) %collective-permute-start.2) | collective-permute-done | bytes 983072 | tf_op jit(solution)/shard_map/ppermute | solution.py:58
  88.1 3.4 %fusion.32 = bf16[2,3,128,128]{3,2,1,0:T(8,128)(2,1)S(1)} fusion(bf16[1,1,3,5120,128]{4,3,2,1,0:T(8,128)(2,1)S(1)} %copy-done.6, bf16[3,128,5120]{2,1,0:T(8,128)(2,1)} %constant_dynamic-update-slice_fusion.8), kind=kOutput, calls=%fused_computation.46 | convolution fusion | flops 1006731264 | bytes 6750208 | tf_op jit(solution)/shard_map/tsd,cdn->tcsn/dot_general | solution.py:230
  93.2 3.0 %convolution_convert_fusion.1 = bf16[2,128,5120]{2,1,0:T(8,128)(2,1)} fusion(bf16[1,384,5120]{2,1,0:T(8,128)(2,1)S(1)} %pad_bitcast_fusion, bf16[1,384,5120]{2,1,0:T(8,128)(2,1)S(1)} %bitcast.361, bf16[1,128,384]{1,2,0:T(8,128)(2,1)S(1)} %pad_bitcast_fusion.2, bf16[1,128,384]{1,2,0:T(8,128)(2,1)S(1)} %bitcast.375), kind=kOutput, calls=%fused_computation.5 | convolution fusion | flops 1011974144 | bytes 10682368 | tf_op jit(solution)/shard_map/tsk,tkd->tsd/dot_general | solution.py:149
  98.3 3.5 %stack.115 = bf16[2,128,5120]{2,1,0:T(8,128)(2,1)} slice(bf16[3,128,5120]{2,1,0:T(8,128)(2,1)} %constant_dynamic-update-slice_fusion.8), slice={[0:2], [0:128], [0:5120]} | slice | bytes 5242880 | tf_op jit(solution)/shard_map/stack | solution.py:229
  102.9 46.0 %reduce-scatter.3.cloned.1.call-done = bf16[2,32,5120]{2,1,0:T(8,128)(2,1)} async-done(((bf16[2,128,5120]{2,1,0:T(8,128)(2,1)}), bf16[2,32,5120]{2,1,0:T(8,128)(2,1)}) %reduce-scatter.3.cloned.1.call-update) | async-done | bytes 655376 | tf_op jit(solution)/shard_map/reduce_scatter | solution.py:263
  150.5 3.3 %collective-permute-start.4 = (bf16[1,32,5120]{2,1,0:T(8,128)(2,1)}, bf16[1,32,5120]{2,1,0:T(8,128)(2,1)S(1)}, u32[]{:S(2)}, u32[]{:S(2)}) collective-permute-start(bf16[1,32,5120]{2,1,0:T(8,128)(2,1)} %bitcast.50), channel_id=1, source_target_pairs={{0,6},{2,0},{4,2},{6,4},{1,7},{3,1},{5,3},{7,5},{8,14},{10,8},{12,... | collective-permute-start | bytes 983048 | tf_op jit(solution)/shard_map/ppermute | solution.py:63
  158.0 4.6 %collective-permute-start.8 = (bf16[32,5120]{1,0:T(8,128)(2,1)S(1)}, bf16[32,5120]{1,0:T(8,128)(2,1)S(1)}, u32[]{:S(2)}, u32[]{:S(2)}) collective-permute-start(bf16[32,5120]{1,0:T(8,128)(2,1)S(1)} %fusion.89), channel_id=1, source_target_pairs={{0,8},{8,16},{9,1},{16,24},{17,9},{25,17},{2,10},{10,18},{11,3},{1... | collective-permute-start | bytes 983048 | tf_op jit(solution)/shard_map/ppermute | solution.py:278
  162.7 5.0 %collective-permute-start.5 = (bf16[1,32,5120]{2,1,0:T(8,128)(2,1)S(1)}, bf16[1,32,5120]{2,1,0:T(8,128)(2,1)S(1)}, u32[]{:S(2)}, u32[]{:S(2)}) collective-permute-start(bf16[1,32,5120]{2,1,0:T(8,128)(2,1)S(1)} %collective-permute-done.3), channel_id=1, source_target_pairs={{0,2},{2,4},{4,6},{6,0},{1,3},{3,5},{5,7},{7,1},{8,10},{10,12},{12... | collective-permute-start | bytes 983048 | tf_op jit(solution)/shard_map/ppermute | solution.py:58
  167.8 7.4 %collective-permute-done.5 = bf16[1,32,5120]{2,1,0:T(8,128)(2,1)S(1)} collective-permute-done((bf16[1,32,5120]{2,1,0:T(8,128)(2,1)S(1)}, bf16[1,32,5120]{2,1,0:T(8,128)(2,1)S(1)}, u32[]{:S(2)}, u32[]{:S(2)}) %collective-permute-start.5) | collective-permute-done | bytes 327712 | tf_op jit(solution)/shard_map/ppermute | solution.py:58
  181.4 2.6 collective-permute-start.12
  184.0 11.8 %collective-permute-done.9 = bf16[2,32,5120]{2,1,0:T(8,128)(2,1)S(1)} collective-permute-done((bf16[2,32,5120]{2,1,0:T(8,128)(2,1)S(1)}, bf16[2,32,5120]{2,1,0:T(8,128)(2,1)S(1)}, u32[]{:S(2)}, u32[]{:S(2)}) %collective-permute-start.9) | collective-permute-done | bytes 655392 | tf_op jit(solution)/shard_map/ppermute | solution.py:58
  195.8 14.0 %collective-permute-done.10 = bf16[2,32,5120]{2,1,0:T(8,128)(2,1)S(1)} collective-permute-done((bf16[2,32,5120]{2,1,0:T(8,128)(2,1)S(1)}, bf16[2,32,5120]{2,1,0:T(8,128)(2,1)S(1)}, u32[]{:S(2)}, u32[]{:S(2)}) %collective-permute-start.10) | collective-permute-done | bytes 655392 | tf_op jit(solution)/shard_map/ppermute | solution.py:63
  209.9 13.8 %collective-permute-done.11 = bf16[2,32,5120]{2,1,0:T(8,128)(2,1)S(1)} collective-permute-done((bf16[2,32,5120]{2,1,0:T(8,128)(2,1)S(1)}, bf16[2,32,5120]{2,1,0:T(8,128)(2,1)S(1)}, u32[]{:S(2)}, u32[]{:S(2)}) %collective-permute-start.11) | collective-permute-done | bytes 655392 | tf_op jit(solution)/shard_map/ppermute | solution.py:58
  228.0 3.0 %convolution_convert_fusion = bf16[2,128,5120]{2,1,0:T(8,128)(2,1)} fusion(bf16[1,384,5120]{2,1,0:T(8,128)(2,1)S(1)} %copy-done.5, bf16[1,384,5120]{2,1,0:T(8,128)(2,1)S(1)} %bitcast.362, bf16[1,128,384]{1,2,0:T(8,128)(2,1)S(1)} %pad_bitcast_fusion.1, bf16[1,128,384]{1,2,0:T(8,128)(2,1)S(1)} %bitcast.374), kind=kOutput, calls=%fused_computation.4 | convolution fusion | flops 1011974144 | bytes 10682368 | tf_op jit(solution)/shard_map/tsk,tkd->tsd/dot_general | solution.py:149
  231.3 3.1 %slice_bitcast_fusion.6 = bf16[128,5120]{1,0:T(8,128)(2,1)} fusion(bf16[2,128,5120]{2,1,0:T(8,128)(2,1)} %copy-done.8), kind=kLoop, calls=%fused_computation.32 | loop fusion | bytes 2621440 | tf_op jit(solution)/shard_map/squeeze | solution.py:68
  245.3 4.4 %fusion = bf16[1,1,3,5120,128]{3,4,2,1,0:T(8,128)(2,1)} fusion(bf16[3,128,5120]{2,1,0:T(8,128)(2,1)S(1)} %add_convert_fusion.1, f32[3,128,5120]{2,1,0:T(8,128)S(1)} %fusion.23, bf16[3,128,5120]{2,1,0:T(8,128)(2,1)} %constant_dynamic-update-slice_fusion.8, bf16[1,128,1,128]{1,3,2,0:T(8,128)(2,1)S(1)} %copy-done.34, bf16[1,128,1,128]{1,3,2,0:T(8,128)(2,1)S(1)} %fusion.59, ...), kind=kOutput, calls=%fused_computation.6 | convolution fusion | flops 515211264 | bytes 17137664 | tf_op jit(solution)/shard_map/sd,csn->cdn/dot_general | solution.py:159
  249.7 6.3 %copy.18 = bf16[1,1,3,5120,128]{4,3,2,1,0:T(8,128)(2,1)} copy(bf16[1,1,3,5120,128]{3,4,2,1,0:T(8,128)(2,1)} %fusion) | data formatting | bytes 7864320
  256.0 10.3 %collective-permute-done.15 = bf16[128,5120]{1,0:T(8,128)(2,1)} collective-permute-done((bf16[128,5120]{1,0:T(8,128)(2,1)}, bf16[128,5120]{1,0:T(8,128)(2,1)}, u32[]{:S(2)}, u32[]{:S(2)}) %collective-permute-start.15) | collective-permute-done | bytes 1310752 | tf_op jit(solution)/shard_map/ppermute | solution.py:18
  268.1 3.1 %fusion.7 = bf16[1,1,128,5120]{3,2,1,0:T(8,128)(2,1)} fusion(f32[128,5120]{1,0:T(8,128)S(1)} %fusion.3, f32[128,5120]{1,0:T(8,128)S(1)} %copy-done.10, bf16[3,128,5120]{2,1,0:T(8,128)(2,1)} %constant_dynamic-update-slice_fusion.8, bf16[128,128]{1,0:T(8,128)(2,1)S(1)} %copy-done.36), kind=kOutput, calls=%fused_computation.15 | convolution fusion | flops 171048960 | bytes 7897088 | tf_op jit(solution)/shard_map/sn,sd->nd/dot_general | solution.py:162
  271.3 8.6 %reduce-scatter.5.cloned.1.call-done = bf16[2,32,5120]{2,1,0:T(8,128)(2,1)} async-done(((bf16[2,128,5120]{2,1,0:T(8,128)(2,1)}), bf16[2,32,5120]{2,1,0:T(8,128)(2,1)}) %reduce-scatter.5.cloned.1.call-update) | async-done | bytes 655376 | tf_op jit(solution)/shard_map/reduce_scatter | solution.py:263
  (182 shorter events, 58.8 us)
Async XLA Ops:
  7.2 141.7 %reduce-scatter.3.cloned.1.call-start = ((), (), s32[]{:S(2)}) async-start(), calls=%async_computation.2 | async-start | bytes 3276800 | tf_op jit(solution)/shard_map/reduce_scatter | solution.py:263
  16.9 28.1 %collective-permute-start = (bf16[3,32,5120]{2,1,0:T(8,128)(2,1)}, bf16[3,32,5120]{2,1,0:T(8,128)(2,1)}, u32[]{:S(2)}, u32[]{:S(2)}) collective-permute-start(bf16[3,32,5120]{2,1,0:T(8,128)(2,1)} %get-tuple-element.32), channel_id=1, source_target_pairs={{0,2},{2,4},{4,6},{6,0},{1,3},{3,5},{5,7},{7,1},{8,10},{10,12},{12... | collective-permute-start | bytes 2949128 | tf_op jit(solution)/shard_map/ppermute | solution.py:58
  20.0 44.8 %collective-permute-start.1 = (bf16[3,32,5120]{2,1,0:T(8,128)(2,1)}, bf16[3,32,5120]{2,1,0:T(8,128)(2,1)}, u32[]{:S(2)}, u32[]{:S(2)}) collective-permute-start(bf16[3,32,5120]{2,1,0:T(8,128)(2,1)} %get-tuple-element.32), channel_id=1, source_target_pairs={{0,6},{2,0},{4,2},{6,4},{1,7},{3,1},{5,3},{7,5},{8,14},{10,8},{12,... | collective-permute-start | bytes 2949128 | tf_op jit(solution)/shard_map/ppermute | solution.py:63
  29.0 64.2 %copy-start.4 = (bf16[1,384,5120]{2,1,0:T(8,128)(2,1)}, bf16[1,384,5120]{2,1,0:T(8,128)(2,1)S(1)}, u32[]{:S(2)}) copy-start(bf16[1,384,5120]{2,1,0:T(8,128)(2,1)S(1)} %pad_bitcast_fusion) | copy-start | bytes 11796484
  45.0 40.2 %collective-permute-start.2 = (bf16[3,32,5120]{2,1,0:T(8,128)(2,1)}, bf16[3,32,5120]{2,1,0:T(8,128)(2,1)S(1)}, u32[]{:S(2)}, u32[]{:S(2)}) collective-permute-start(bf16[3,32,5120]{2,1,0:T(8,128)(2,1)} %collective-permute-done), channel_id=1, source_target_pairs={{0,2},{2,4},{4,6},{6,0},{1,3},{3,5},{5,7},{7,1},{8,10},{10,12},{12... | collective-permute-start | bytes 2949128 | tf_op jit(solution)/shard_map/ppermute | solution.py:58
  67.0 21.1 %copy-start.6 = (bf16[1,1,3,5120,128]{4,3,2,1,0:T(8,128)(2,1)S(1)}, bf16[1,1,3,5120,128]{4,3,2,1,0:T(8,128)(2,1)}, u32[]{:S(2)}) copy-start(bf16[1,1,3,5120,128]{4,3,2,1,0:T(8,128)(2,1)} %param.16) | copy-start | bytes 11796484
  96.2 183.6 %reduce-scatter.5.cloned.1.call-start = ((), (), s32[]{:S(2)}) async-start(), calls=%async_computation.3 | async-start | bytes 3276800 | tf_op jit(solution)/shard_map/reduce_scatter | solution.py:263
  101.8 53.5 %copy-start.24 = (bf16[1,1,32,5120]{3,2,1,0:T(8,128)(2,1)S(1)}, bf16[1,1,32,5120]{3,2,1,0:T(8,128)(2,1)}, u32[]{:S(2)}) copy-start(bf16[1,1,32,5120]{3,2,1,0:T(8,128)(2,1)} %param.19) | copy-start | bytes 983044
  101.8 73.4 %collective-permute-start.6 = (bf16[2,128,5120]{2,1,0:T(8,128)(2,1)}, bf16[2,128,5120]{2,1,0:T(8,128)(2,1)}, u32[]{:S(2)}, u32[]{:S(2)}) collective-permute-start(bf16[2,128,5120]{2,1,0:T(8,128)(2,1)} %stack.115), channel_id=1, source_target_pairs={{0,25},{1,24},{8,17},{9,16},{16,9},{17,8},{24,1},{25,0},{2,27},{3,... | collective-permute-start | bytes 7864328 | tf_op jit(solution)/shard_map/ppermute | solution.py:18
  102.3 55.7 %copy-start.35 = (bf16[128,128]{1,0:T(8,128)(2,1)}, bf16[128,128]{1,0:T(8,128)(2,1)S(1)}, u32[]{:S(2)}) copy-start(bf16[128,128]{1,0:T(8,128)(2,1)S(1)} %convolution_convert_fusion.8) | copy-start | bytes 98308
  150.0 12.7 %collective-permute-start.3 = (bf16[1,32,5120]{2,1,0:T(8,128)(2,1)}, bf16[1,32,5120]{2,1,0:T(8,128)(2,1)S(1)}, u32[]{:S(2)}, u32[]{:S(2)}) collective-permute-start(bf16[1,32,5120]{2,1,0:T(8,128)(2,1)} %bitcast.50), channel_id=1, source_target_pairs={{0,2},{2,4},{4,6},{6,0},{1,3},{3,5},{5,7},{7,1},{8,10},{10,12},{12... | collective-permute-start | bytes 983048 | tf_op jit(solution)/shard_map/ppermute | solution.py:58
  150.5 17.2 %collective-permute-start.4 = (bf16[1,32,5120]{2,1,0:T(8,128)(2,1)}, bf16[1,32,5120]{2,1,0:T(8,128)(2,1)S(1)}, u32[]{:S(2)}, u32[]{:S(2)}) collective-permute-start(bf16[1,32,5120]{2,1,0:T(8,128)(2,1)} %bitcast.50), channel_id=1, source_target_pairs={{0,6},{2,0},{4,2},{6,4},{1,7},{3,1},{5,3},{7,5},{8,14},{10,8},{12,... | collective-permute-start | bytes 983048 | tf_op jit(solution)/shard_map/ppermute | solution.py:63
  155.3 20.3 %copy-start.16 = (bf16[1,2,32,5120]{3,2,1,0:T(8,128)(2,1)S(1)}, bf16[1,2,32,5120]{3,2,1,0:T(8,128)(2,1)}, u32[]{:S(2)}) copy-start(bf16[1,2,32,5120]{3,2,1,0:T(8,128)(2,1)} %param.21) | copy-start | bytes 1966084
  156.6 18.7 %collective-permute-start.7 = (bf16[32,5120]{1,0:T(8,128)(2,1)S(1)}, bf16[32,5120]{1,0:T(8,128)(2,1)S(1)}, u32[]{:S(2)}, u32[]{:S(2)}) collective-permute-start(bf16[32,5120]{1,0:T(8,128)(2,1)S(1)} %fusion.77), channel_id=1, source_target_pairs={{1,9},{8,0},{9,17},{16,8},{17,25},{24,16},{3,11},{10,2},{11,19},{1... | collective-permute-start | bytes 983048 | tf_op jit(solution)/shard_map/ppermute | solution.py:277
  158.0 17.3 %collective-permute-start.8 = (bf16[32,5120]{1,0:T(8,128)(2,1)S(1)}, bf16[32,5120]{1,0:T(8,128)(2,1)S(1)}, u32[]{:S(2)}, u32[]{:S(2)}) collective-permute-start(bf16[32,5120]{1,0:T(8,128)(2,1)S(1)} %fusion.89), channel_id=1, source_target_pairs={{0,8},{8,16},{9,1},{16,24},{17,9},{25,17},{2,10},{10,18},{11,3},{1... | collective-permute-start | bytes 983048 | tf_op jit(solution)/shard_map/ppermute | solution.py:278
  162.7 12.5 %collective-permute-start.5 = (bf16[1,32,5120]{2,1,0:T(8,128)(2,1)S(1)}, bf16[1,32,5120]{2,1,0:T(8,128)(2,1)S(1)}, u32[]{:S(2)}, u32[]{:S(2)}) collective-permute-start(bf16[1,32,5120]{2,1,0:T(8,128)(2,1)S(1)} %collective-permute-done.3), channel_id=1, source_target_pairs={{0,2},{2,4},{4,6},{6,0},{1,3},{3,5},{5,7},{7,1},{8,10},{10,12},{12... | collective-permute-start | bytes 983048 | tf_op jit(solution)/shard_map/ppermute | solution.py:58
  176.3 19.5 %collective-permute-start.9 = (bf16[2,32,5120]{2,1,0:T(8,128)(2,1)S(1)}, bf16[2,32,5120]{2,1,0:T(8,128)(2,1)S(1)}, u32[]{:S(2)}, u32[]{:S(2)}) collective-permute-start(bf16[2,32,5120]{2,1,0:T(8,128)(2,1)S(1)} %get-tuple-element.36), channel_id=1, source_target_pairs={{0,2},{2,4},{4,6},{6,0},{1,3},{3,5},{5,7},{7,1},{8,10},{10,12},{12... | collective-permute-start | bytes 1966088 | tf_op jit(solution)/shard_map/ppermute | solution.py:58
  178.7 45.0 %copy-start.19 = (bf16[1,1,128,5120]{3,2,1,0:T(8,128)(2,1)S(1)}, bf16[1,1,128,5120]{3,2,1,0:T(8,128)(2,1)}, u32[]{:S(2)}) copy-start(bf16[1,1,128,5120]{3,2,1,0:T(8,128)(2,1)} %param.17) | copy-start | bytes 3932164
  178.7 31.1 %collective-permute-start.10 = (bf16[2,32,5120]{2,1,0:T(8,128)(2,1)S(1)}, bf16[2,32,5120]{2,1,0:T(8,128)(2,1)S(1)}, u32[]{:S(2)}, u32[]{:S(2)}) collective-permute-start(bf16[2,32,5120]{2,1,0:T(8,128)(2,1)S(1)} %get-tuple-element.36), channel_id=1, source_target_pairs={{0,6},{2,0},{4,2},{6,4},{1,7},{3,1},{5,3},{7,5},{8,14},{10,8},{12,... | collective-permute-start | bytes 1966088 | tf_op jit(solution)/shard_map/ppermute | solution.py:63
  181.3 49.7 %collective-permute-start.13 = (bf16[4,128,128]{1,2,0:T(8,128)(2,1)}, bf16[4,128,128]{1,2,0:T(8,128)(2,1)}, u32[]{:S(2)}, u32[]{:S(2)}) collective-permute-start(bf16[4,128,128]{1,2,0:T(8,128)(2,1)} %pad_maximum_fusion.5), channel_id=1, source_target_pairs={{0,25},{1,24},{8,17},{9,16},{16,9},{17,8},{24,1},{25,0},{2,27},{3,... | collective-permute-start | bytes 393224 | tf_op jit(solution)/shard_map/ppermute | solution.py:18
  181.4 49.6 %collective-permute-start.12 = (bf16[1,128,5120]{2,1,0:T(8,128)(2,1)S(1)}, bf16[1,128,5120]{2,1,0:T(8,128)(2,1)S(1)}, u32[]{:S(2)}, u32[]{:S(2)}) collective-permute-start(bf16[1,128,5120]{2,1,0:T(8,128)(2,1)S(1)} %constant_dynamic-update-slice_fusion.4), channel_id=1, source_target_pairs={{0,25},{1,24},{8,17},{9,16},{16,9},{17,8},{24,1},{25,0},{2,27},{3,... | collective-permute-start | bytes 3932168 | tf_op jit(solution)/shard_map/ppermute | solution.py:18
  195.8 27.9 %collective-permute-start.11 = (bf16[2,32,5120]{2,1,0:T(8,128)(2,1)S(1)}, bf16[2,32,5120]{2,1,0:T(8,128)(2,1)S(1)}, u32[]{:S(2)}, u32[]{:S(2)}) collective-permute-start(bf16[2,32,5120]{2,1,0:T(8,128)(2,1)S(1)} %collective-permute-done.9), channel_id=1, source_target_pairs={{0,2},{2,4},{4,6},{6,0},{1,3},{3,5},{5,7},{7,1},{8,10},{10,12},{12... | collective-permute-start | bytes 1966088 | tf_op jit(solution)/shard_map/ppermute | solution.py:58
  231.2 10.3 %collective-permute-start.14 = (bf16[4,128,128]{1,2,0:T(8,128)(2,1)S(1)}, bf16[4,128,128]{1,2,0:T(8,128)(2,1)S(1)}, u32[]{:S(2)}, u32[]{:S(2)}) collective-permute-start(bf16[4,128,128]{1,2,0:T(8,128)(2,1)S(1)} %pad_maximum_fusion.6), channel_id=1, source_target_pairs={{0,25},{1,24},{8,17},{9,16},{16,9},{17,8},{24,1},{25,0},{2,27},{3,... | collective-permute-start | bytes 393224 | tf_op jit(solution)/shard_map/ppermute | solution.py:18
  234.4 31.9 %collective-permute-start.15 = (bf16[128,5120]{1,0:T(8,128)(2,1)}, bf16[128,5120]{1,0:T(8,128)(2,1)}, u32[]{:S(2)}, u32[]{:S(2)}) collective-permute-start(bf16[128,5120]{1,0:T(8,128)(2,1)} %slice_bitcast_fusion.6), channel_id=1, source_target_pairs={{0,25},{1,24},{8,17},{9,16},{16,9},{17,8},{24,1},{25,0},{2,27},{3,... | collective-permute-start | bytes 3932168 | tf_op jit(solution)/shard_map/ppermute | solution.py:18
  (32 other events, 229.2 us)
Sparse Core Ops, SparseCore 0:
  96.3 52.5 reduce-scatter.2
  231.1 48.6 reduce-scatter.4
